TPU v7x, 128 devices: a whole 4x4x4 slice. The times are simulated.
128 devices in a mesh: freq: 8 (over y, core), outp: 8 (over x, z_lo), inp: 2 (over z_hi).
Axes of the slice: x: 4, y: 4, z: 4 (z_hi: 2, z_lo: 2; z = z_hi * 2 + z_lo), core: 2. Of those that a mesh axis runs over, the one named last changes fastest.
Arguments:
- measured: float32 [2, 8, 2048, 2048], P(None, 'freq', 'outp', 'inp'), may hold values from -6 to 6
- left_factor: bfloat16 [2048, 4096], P('outp', 'freq'), may hold values from -0.75 to 0.75
- right_factor: bfloat16 [4096, 2048], P('freq', 'inp'), may hold values from -0.75 to 0.75
- pole_rates: float32 [512], replicated, may hold values from 0.5 to 8
- sample_freqs: float32 [8], P('freq'), may hold values from 0 to 8
Outputs:
- grad_left: float32 [2048, 4096], P('outp', ('freq', 'inp'))
- grad_right: float32 [4096, 2048], P(('freq', 'outp'), 'inp')
All inputs are finite; a program needn't handle non-finite values.
Results may differ from a plain program's by a relative error of at most 0.0003.
Values may be sent and summed in bfloat16 or wider, within the bound.
No kernel may reach another device: no remote copies, remote signals or barrier semaphores. Data moves between devices by JAX's collectives and lax.ppermute only.
A program may use at most 128 MiB of HBM per device.

v0:
```python
import math
import jax
import jax.numpy as jnp
from jax import lax
from jax.sharding import PartitionSpec as P

PORTS = 2048
RANK = 8
RANKS = 4096


def shards(measured, left_factor, right_factor, pole_rates, sample_freqs):
    highest = lax.Precision.HIGHEST
    left_whole = lax.all_gather(left_factor, "freq", axis=1, tiled=True)
    right_whole = lax.all_gather(right_factor, "freq", axis=0, tiled=True)
    local_samples = sample_freqs.shape[0]
    out_rows = left_whole.shape[0]
    in_cols = right_whole.shape[1]
    total_samples = local_samples * lax.axis_size("freq")
    grad_scale = float(RANKS) ** 0.25 / math.sqrt(float(total_samples * PORTS))
    left_wide = left_whole.astype(jnp.float32)
    right_wide = right_whole.astype(jnp.float32)
    omega = sample_freqs[0]
    denominator = pole_rates * pole_rates + omega * omega
    real_resp = jnp.repeat(pole_rates / denominator, RANK)
    imag_resp = jnp.repeat(-omega / denominator, RANK)
    scaled = jnp.concatenate([left_wide * real_resp[None, :], left_wide * imag_resp[None, :]], 0)
    fitted = jnp.dot(scaled, right_wide, precision=highest, preferred_element_type=jnp.float32)
    observed = measured[:, 0].reshape(2 * out_rows, in_cols)
    misfit = fitted - observed
    backward = lax.dot_general(
        misfit,
        right_wide,
        (((1,), (1,)), ((), ())),
        precision=highest,
        preferred_element_type=jnp.float32,
    )
    left_acc = backward[:out_rows] * real_resp[None, :] + backward[out_rows:] * imag_resp[None, :]
    left_term = left_acc * grad_scale
    grad_left = lax.psum_scatter(left_term, ("freq", "inp"), scatter_dimension=1, tiled=True)
    product = lax.dot_general(
        scaled,
        misfit,
        (((0,), (0,)), ((), ())),
        precision=highest,
        preferred_element_type=jnp.float32,
    )
    grad_right = lax.psum_scatter(
        product * grad_scale, ("freq", "outp"), scatter_dimension=0, tiled=True
    )
    return (grad_left, grad_right)


def solution(mesh):
    return jax.shard_map(
        shards,
        mesh=mesh,
        in_specs=(
            P(None, "freq", "outp", "inp"),
            P("outp", "freq"),
            P("freq", "inp"),
            P(),
            P("freq"),
        ),
        out_specs=(P("outp", ("freq", "inp")), P(("freq", "outp"), "inp")),
        check_vma=False,
    )
```

profile of v0, /device:TPU:1, one launch (start us, length us, event | category | flops | bytes accessed | tf_op | source)
XLA Modules:
  0.0 579.0 jit_solution(4097242679479421879)
XLA Ops:
  7.2 0.0 all-gather.3.cloned.1.call-start
  7.2 0.7 all-gather.3.cloned.1.call-update
  7.9 0.0 all-gather.5.cloned.1.call-start
  7.9 0.7 all-gather.5.cloned.1.call-update
  8.6 0.0 reduce-scatter.3.cloned.1.call-start
  9.3 0.7 fusion.5
  10.0 0.1 broadcast_in_dim.6
  10.2 0.2 mul.56
  10.3 0.1 broadcast_in_dim.7
  10.4 0.2 mul.59
  10.6 28.0 %all-gather.3.cloned.1.call-done = bf16[256,4096]{1,0:T(8,128)(2,1)} async-done(((bf16[256,512]{1,0:T(8,128)(2,1)}), bf16[256,4096]{1,0:T(8,128)(2,1)}) %all-gather.3.cloned.1.call-update) | async-done | bytes 2097168 | tf_op jit(solution)/shard_map/all_gather | solution.py:14
  38.6 5.9 %convert_multiply_fusion.1 = (f32[256,4096]{1,0:T(8,128)}, f32[256,4096]{1,0:T(8,128)}) fusion(bf16[256,4096]{1,0:T(8,128)(2,1)} %all-gather.3.cloned.1.call-done, f32[4096]{0:T(1024)S(1)} %mul.56, f32[4096]{0:T(1024)S(1)} %mul.59), kind=kLoop, calls=%fused_computation.5 | loop fusion | flops 3145728 | bytes 10518528 | tf_op jit(solution)/shard_map/mul | solution.py:27
  44.5 45.9 %all-gather.5.cloned.1.call-done = bf16[4096,1024]{1,0:T(8,128)(2,1)} async-done(((bf16[512,1024]{1,0:T(8,128)(2,1)}), bf16[4096,1024]{1,0:T(8,128)(2,1)}) %all-gather.5.cloned.1.call-update) | async-done | bytes 8388624 | tf_op jit(solution)/shard_map/all_gather | solution.py:15
  90.3 0.0 copy-start
  90.3 17.0 %bitcast_subtract_fusion = f32[512,1024]{1,0:T(8,128)S(1)} fusion(f32[2,1,256,1024]{3,2,1,0:T(8,128)} %param.5, bf16[4096,1024]{1,0:T(8,128)(2,1)} %all-gather.5.cloned.1.call-done, f32[256,4096]{1,0:T(8,128)} %get-tuple-element.3, f32[256,4096]{1,0:T(8,128)} %get-tuple-element.2), kind=kOutput, calls=%fused_computation.10 | convolution fusion | flops 25772425216 | bytes 20971520 | tf_op jit(solution)/shard_map/dot_general | solution.py:28
  107.4 0.0 copy-done
  107.4 13.6 %fusion.8 = f32[512,4096]{1,0:T(8,128)S(1)} fusion(f32[512,1024]{1,0:T(8,128)S(1)} %bitcast_subtract_fusion, bf16[4096,1024]{1,0:T(8,128)(2,1)S(1)} %copy-done), kind=kOutput, calls=%fused_computation.16 | convolution fusion | flops 25769803776 | bytes 18874368 | tf_op jit(solution)/shard_map/dot_general | solution.py:31
  121.0 2.8 fusion.3
  123.7 0.0 reduce-scatter.3.cloned.1.call-update
  123.8 0.2 reduce-scatter.5.cloned.1.call-start
  124.0 30.7 %broadcast_multiply_fusion = f32[4096,1024]{1,0:T(8,128)} fusion(f32[512,1024]{1,0:T(8,128)S(1)} %bitcast_subtract_fusion, f32[256,4096]{1,0:T(8,128)} %get-tuple-element.3, f32[256,4096]{1,0:T(8,128)} %get-tuple-element.2), kind=kOutput, calls=%fused_computation.1 | convolution fusion | flops 25776095232 | bytes 27262976 | tf_op jit(solution)/shard_map/dot_general | solution.py:41
  154.7 0.0 reduce-scatter.5.cloned.1.call-update
  154.7 48.2 %reduce-scatter.3.cloned.1.call-done = f32[256,256]{1,0:T(8,128)} async-done(((f32[256,4096]{1,0:T(8,128)}), f32[256,256]{1,0:T(8,128)}) %reduce-scatter.3.cloned.1.call-update) | async-done | bytes 262160 | tf_op jit(solution)/shard_map/reduce_scatter | solution.py:40
  202.9 369.6 %reduce-scatter.5.cloned.1.call-done = f32[64,1024]{1,0:T(8,128)} async-done(((f32[4096,1024]{1,0:T(8,128)}), f32[64,1024]{1,0:T(8,128)}) %reduce-scatter.5.cloned.1.call-update) | async-done | bytes 262160 | tf_op jit(solution)/shard_map/reduce_scatter | solution.py:48
Async XLA Ops:
  7.2 31.4 %all-gather.3.cloned.1.call-start = ((), (), s32[]{:S(2)}) async-start(), calls=%async_computation.2 | async-start | bytes 2359296 | tf_op jit(solution)/shard_map/all_gather | solution.py:14
  7.9 82.4 %all-gather.5.cloned.1.call-start = ((), (), s32[]{:S(2)}) async-start(), calls=%async_computation.3 | async-start | bytes 9437184 | tf_op jit(solution)/shard_map/all_gather | solution.py:15
  8.6 194.3 %reduce-scatter.3.cloned.1.call-start = ((), (), s32[]{:S(2)}) async-start(), calls=%async_computation.4 | async-start | bytes 4456448 | tf_op jit(solution)/shard_map/reduce_scatter | solution.py:40
  90.3 17.0 %copy-start = (bf16[4096,1024]{1,0:T(8,128)(2,1)S(1)}, bf16[4096,1024]{1,0:T(8,128)(2,1)}, u32[]{:S(2)}) copy-start(bf16[4096,1024]{1,0:T(8,128)(2,1)} %all-gather.5.cloned.1.call-done) | copy-start | bytes 25165828
  123.8 448.7 %reduce-scatter.5.cloned.1.call-start = ((), (), s32[]{:S(2)}) async-start(), calls=%async_computation.5 | async-start | bytes 17039360 | tf_op jit(solution)/shard_map/reduce_scatter | solution.py:48
Sparse Core Ops, SparseCore 0:
  9.7 28.8 all-gather.2
  40.3 49.9 all-gather.4
  123.9 78.9 reduce-scatter.2
  205.7 366.7 reduce-scatter.4
where the time goes:
time: 579 us
  waiting for transfers between devices  493 us (85%)
  matrix products  61.3 us (11%)
  between operations  14.5 us (3%)
  other arithmetic  9.32 us (2%)
    reduce_scatter x1, waiting for transfers between devices, shards(): lax.psum_scatter(product * grad_scale, ('freq', 'outp'), scatter_dimensio...  370 us
    reduce_scatter x1, waiting for transfers between devices, shards(): lax.psum_scatter(left_term, ('freq', 'inp'), scatter_dimension=1, tiled=T...  48.2 us
    all_gather x1, waiting for transfers between devices, shards(): right_whole = lax.all_gather(right_factor, 'freq', axis=0, tiled=True)  45.9 us
    dot_general x1, matrix products, shards(): lax.dot_general(scaled, misfit, (((0,), (0,)), ((), ())), precision=highe...  30.7 us
    all_gather x1, waiting for transfers between devices, shards(): left_whole = lax.all_gather(left_factor, 'freq', axis=1, tiled=True)  28 us
    dot_general x1, matrix products, shards(): jnp.dot(scaled, right_wide, precision=highest, preferred_element_type=jnp...  17 us
    dot_general x1, matrix products, shards(): lax.dot_general(misfit, right_wide, (((1,), (1,)), ((), ())), precision=h...  13.6 us
  transfers between devices with their start and end apart: 4, of which 4 were waited for; matrix products, arithmetic and copies ran while one was open for 7% of the time, Pallas kernels for 0%

commit v1 on v0

--- a/solution.py
+++ b/solution.py
@@ -12,7 +12,18 @@
 def shards(measured, left_factor, right_factor, pole_rates, sample_freqs):
     highest = lax.Precision.HIGHEST
     left_whole = lax.all_gather(left_factor, "freq", axis=1, tiled=True)
-    right_whole = lax.all_gather(right_factor, "freq", axis=0, tiled=True)
+    ways = lax.axis_size("freq")
+    up = [(d, (d + 1) % ways) for d in range(ways)]
+    down = [(d, (d - 1) % ways) for d in range(ways)]
+    earlier, later = ([right_factor], [right_factor])
+    for _ in range(ways // 2):
+        earlier.append(lax.ppermute(earlier[-1], "freq", up))
+    for _ in range((ways - 1) // 2):
+        later.append(lax.ppermute(later[-1], "freq", down))
+    line = jnp.concatenate([*earlier[::-1], *later[1:]], axis=0)
+    right_whole = jnp.roll(
+        line, (lax.axis_index("freq") - ways // 2) * right_factor.shape[0], axis=0
+    )
     local_samples = sample_freqs.shape[0]
     out_rows = left_whole.shape[0]
     in_cols = right_whole.shape[1]

time: 579 us -> 577 us (level)
  waiting for transfers between devices: 493 us -> 469 us
  local copies, waits for them, and re-layouts: 0.55 us -> 13.9 us
  starting transfers between devices: 0.34 us -> 13.5 us
    ppermute x0 -> x7, waiting for transfers between devices: none -> 46 us  [the longest x4 46 us: shards(): earlier.append(lax.ppermute(earlier[-1], 'freq', up))]
    all_gather x1 -> x0, waiting for transfers between devices: 45.9 us -> none  [shards(): right_whole = lax.all_gather(right_factor, 'freq', axis=0, tiled=True)]
    all_gather x1, waiting for transfers between devices: 28 us -> 0.01 us  [shards(): left_whole = lax.all_gather(left_factor, 'freq', axis=1, tiled=True)]
    ppermute x0 -> x7, starting transfers between devices: none -> 13.4 us  [the longest x4 10.1 us: shards(): earlier.append(lax.ppermute(earlier[-1], 'freq', up))]
    unnamed x2 -> x23, local copies, waits for them, and re-layouts: 0.01 us -> 12.1 us
  transfers between devices with their start and end apart: 4 -> 10, of which waited for: 4 -> 6; matrix products, arithmetic and copies ran while one was open for 7% -> 7% of each run, Pallas kernels for 0% -> 0%
where the time goes in v1:
time: 577 us
  waiting for transfers between devices  469 us (81%)
  matrix products  59.1 us (10%)
  between operations  14.6 us (3%)
  local copies, waits for them, and re-layouts  13.9 us (2%)
  starting transfers between devices  13.5 us (2%)
  other arithmetic  6.08 us (1%)
    reduce_scatter x1, waiting for transfers between devices, shards(): lax.psum_scatter(product * grad_scale, ('freq', 'outp'), scatter_dimensio...  370 us
    reduce_scatter x1, waiting for transfers between devices, shards(): lax.psum_scatter(left_term, ('freq', 'inp'), scatter_dimension=1, tiled=T...  53 us
    ppermute x4, waiting for transfers between devices, shards(): earlier.append(lax.ppermute(earlier[-1], 'freq', up))  46 us
    dot_general x1, matrix products, shards(): lax.dot_general(scaled, misfit, (((0,), (0,)), ((), ())), precision=highe...  30.9 us
    dot_general x1, matrix products, shards(): jnp.dot(scaled, right_wide, precision=highest, preferred_element_type=jnp...  14.4 us
    dot_general x1, matrix products, shards(): lax.dot_general(misfit, right_wide, (((1,), (1,)), ((), ())), precision=h...  13.7 us
    unnamed x23, local copies, waits for them, and re-layouts  12.1 us
  transfers between devices with their start and end apart: 10, of which 6 were waited for; matrix products, arithmetic and copies ran while one was open for 7% of the time, Pallas kernels for 0%

profile of v1, /device:TPU:1, one launch (start us, length us, event | category | flops | bytes accessed | tf_op | source)
XLA Modules:
  0.0 576.7 jit_solution(9243541933164500379)
XLA Ops:
  7.2 0.7 all-gather.2.cloned.1.call-update
  8.0 2.7 collective-permute-start
  10.6 12.1 %collective-permute-done = bf16[512,1024]{1,0:T(8,128)(2,1)S(1)} collective-permute-done((bf16[512,1024]{1,0:T(8,128)(2,1)}, bf16[512,1024]{1,0:T(8,128)(2,1)S(1)}, u32[]{:S(2)}, u32[]{:S(2)}) %collective-permute-start) | collective-permute-done | bytes 1048608 | tf_op jit(solution)/shard_map/ppermute | solution.py:20
  22.7 2.4 collective-permute-start.1
  25.1 1.9 collective-permute-start.5
  27.0 15.8 %collective-permute-done.1 = bf16[512,1024]{1,0:T(8,128)(2,1)} collective-permute-done((bf16[512,1024]{1,0:T(8,128)(2,1)S(1)}, bf16[512,1024]{1,0:T(8,128)(2,1)}, u32[]{:S(2)}, u32[]{:S(2)}) %collective-permute-start.1) | collective-permute-done | bytes 1048608 | tf_op jit(solution)/shard_map/ppermute | solution.py:20
  42.8 2.6 collective-permute-start.2
  46.1 0.7 fusion.10
  46.8 0.1 broadcast_in_dim.6
  46.9 0.2 mul.59
  47.2 0.2 mul.62
  47.3 1.3 collective-permute-start.6
  48.7 8.8 %collective-permute-done.2 = bf16[512,1024]{1,0:T(8,128)(2,1)} collective-permute-done((bf16[512,1024]{1,0:T(8,128)(2,1)}, bf16[512,1024]{1,0:T(8,128)(2,1)}, u32[]{:S(2)}, u32[]{:S(2)}) %collective-permute-start.2) | collective-permute-done | bytes 1048608 | tf_op jit(solution)/shard_map/ppermute | solution.py:20
  57.5 2.5 collective-permute-start.3
  59.9 2.6 convert_multiply_fusion.1
  62.6 9.4 %collective-permute-done.3 = bf16[512,1024]{1,0:T(8,128)(2,1)} collective-permute-done((bf16[512,1024]{1,0:T(8,128)(2,1)}, bf16[512,1024]{1,0:T(8,128)(2,1)}, u32[]{:S(2)}, u32[]{:S(2)}) %collective-permute-start.3) | collective-permute-done | bytes 1048608 | tf_op jit(solution)/shard_map/ppermute | solution.py:20
  72.0 1.3 constant_dynamic-update-slice_fusion.15
  73.3 1.3 constant_dynamic-update-slice_fusion.14
  74.6 1.3 constant_dynamic-update-slice_fusion.13
  76.1 1.3 constant_dynamic-update-slice_fusion.9
  77.4 1.3 constant_dynamic-update-slice_fusion.8
  78.7 1.3 constant_dynamic-update-slice_fusion.7
  80.0 1.3 constant_dynamic-update-slice_fusion.6
  81.3 1.3 constant_dynamic-update-slice_fusion.5
  82.9 1.3 constant_dynamic-update-slice_fusion.1
  84.2 1.3 constant_dynamic-update-slice_fusion
  85.5 14.4 %bitcast_subtract_fusion = f32[512,1024]{1,0:T(8,128)S(1)} fusion(f32[2,1,256,1024]{3,2,1,0:T(8,128)S(1)} %copy-done.3, bf16[8192,1024]{1,0:T(8,128)(2,1)S(1)} %constant_dynamic-update-slice_fusion, s32[]{:T(128)S(6)} %select_n.14, f32[256,4096]{1,0:T(8,128)S(1)} %get-tuple-element.3, f32[256,4096]{1,0:T(8,128)S(1)} %get-tuple-element.2), kind=kOutput, calls=%fused_computation.13 | convolution fusion | flops 25772425216 | bytes 20971524 | tf_op jit(solution)/shard_map/dot_general | solution.py:39
  100.0 13.7 %fusion = f32[512,4096]{1,0:T(8,128)S(1)} fusion(f32[512,1024]{1,0:T(8,128)S(1)} %bitcast_subtract_fusion, bf16[8192,1024]{1,0:T(8,128)(2,1)S(1)} %constant_dynamic-update-slice_fusion, s32[]{:T(128)S(6)} %select_n.14), kind=kOutput, calls=%fused_computation.2 | convolution fusion | flops 25769803776 | bytes 18874372 | tf_op jit(solution)/shard_map/dot_general | solution.py:42
  113.7 2.8 fusion.6
  116.5 30.9 %broadcast_multiply_fusion = f32[4096,1024]{1,0:T(8,128)} fusion(f32[512,1024]{1,0:T(8,128)S(1)} %bitcast_subtract_fusion, f32[256,4096]{1,0:T(8,128)} %copy-done.1, f32[256,4096]{1,0:T(8,128)} %copy-done), kind=kOutput, calls=%fused_computation.1 | convolution fusion | flops 25776095232 | bytes 27262976 | tf_op jit(solution)/shard_map/dot_general | solution.py:52
  147.5 53.0 %reduce-scatter.3.cloned.1.call-done = f32[256,256]{1,0:T(8,128)} async-done(((f32[256,4096]{1,0:T(8,128)}), f32[256,256]{1,0:T(8,128)}) %reduce-scatter.3.cloned.1.call-update) | async-done | bytes 262160 | tf_op jit(solution)/shard_map/reduce_scatter | solution.py:51
  200.4 369.8 %reduce-scatter.5.cloned.1.call-done = f32[64,1024]{1,0:T(8,128)} async-done(((f32[4096,1024]{1,0:T(8,128)}), f32[64,1024]{1,0:T(8,128)}) %reduce-scatter.5.cloned.1.call-update) | async-done | bytes 262160 | tf_op jit(solution)/shard_map/reduce_scatter | solution.py:59
  (25 shorter events, 0.7 us)
Async XLA Ops:
  7.2 68.8 %copy-start.2 = (bf16[512,1024]{1,0:T(8,128)(2,1)S(1)}, bf16[512,1024]{1,0:T(8,128)(2,1)}, u32[]{:S(2)}) copy-start(bf16[512,1024]{1,0:T(8,128)(2,1)} %param.7) | copy-start | bytes 3145732
  7.2 52.8 %all-gather.2.cloned.1.call-start = ((), (), s32[]{:S(2)}) async-start(), calls=%async_computation.2 | async-start | bytes 2359296 | tf_op jit(solution)/shard_map/all_gather | solution.py:14
  7.9 192.5 %reduce-scatter.3.cloned.1.call-start = ((), (), s32[]{:S(2)}) async-start(), calls=%async_computation.3 | async-start | bytes 4456448 | tf_op jit(solution)/shard_map/reduce_scatter | solution.py:51
  8.0 14.7 %collective-permute-start = (bf16[512,1024]{1,0:T(8,128)(2,1)}, bf16[512,1024]{1,0:T(8,128)(2,1)S(1)}, u32[]{:S(2)}, u32[]{:S(2)}) collective-permute-start(bf16[512,1024]{1,0:T(8,128)(2,1)} %param.7), channel_id=1, source_target_pairs={{0,16},{16,32},{32,48},{48,64},{64,80},{80,96},{96,112},{112,0},{1... | collective-permute-start | bytes 3145736 | tf_op jit(solution)/shard_map/ppermute | solution.py:20
  10.6 14.4 %collective-permute-start.4 = (bf16[512,1024]{1,0:T(8,128)(2,1)}, bf16[512,1024]{1,0:T(8,128)(2,1)S(1)}, u32[]{:S(2)}, u32[]{:S(2)}) collective-permute-start(bf16[512,1024]{1,0:T(8,128)(2,1)} %param.7), channel_id=1, source_target_pairs={{0,112},{16,0},{32,16},{48,32},{64,48},{80,64},{96,80},{112,96},{1... | collective-permute-start | bytes 3145736 | tf_op jit(solution)/shard_map/ppermute | solution.py:22
  22.7 20.1 %collective-permute-start.1 = (bf16[512,1024]{1,0:T(8,128)(2,1)S(1)}, bf16[512,1024]{1,0:T(8,128)(2,1)}, u32[]{:S(2)}, u32[]{:S(2)}) collective-permute-start(bf16[512,1024]{1,0:T(8,128)(2,1)S(1)} %collective-permute-done), channel_id=1, source_target_pairs={{0,16},{16,32},{32,48},{48,64},{64,80},{80,96},{96,112},{112,0},{1... | collective-permute-start | bytes 3145736 | tf_op jit(solution)/shard_map/ppermute | solution.py:20
  25.1 22.3 %collective-permute-start.5 = (bf16[512,1024]{1,0:T(8,128)(2,1)S(1)}, bf16[512,1024]{1,0:T(8,128)(2,1)}, u32[]{:S(2)}, u32[]{:S(2)}) collective-permute-start(bf16[512,1024]{1,0:T(8,128)(2,1)S(1)} %collective-permute-done.4), channel_id=1, source_target_pairs={{0,112},{16,0},{32,16},{48,32},{64,48},{80,64},{96,80},{112,96},{1... | collective-permute-start | bytes 3145736 | tf_op jit(solution)/shard_map/ppermute | solution.py:22
  42.8 14.6 %collective-permute-start.2 = (bf16[512,1024]{1,0:T(8,128)(2,1)}, bf16[512,1024]{1,0:T(8,128)(2,1)}, u32[]{:S(2)}, u32[]{:S(2)}) collective-permute-start(bf16[512,1024]{1,0:T(8,128)(2,1)} %collective-permute-done.1), channel_id=1, source_target_pairs={{0,16},{16,32},{32,48},{48,64},{64,80},{80,96},{96,112},{112,0},{1... | collective-permute-start | bytes 3145736 | tf_op jit(solution)/shard_map/ppermute | solution.py:20
  47.3 30.1 %collective-permute-start.6 = (bf16[512,1024]{1,0:T(8,128)(2,1)}, bf16[512,1024]{1,0:T(8,128)(2,1)}, u32[]{:S(2)}, u32[]{:S(2)}) collective-permute-start(bf16[512,1024]{1,0:T(8,128)(2,1)} %collective-permute-done.5), channel_id=1, source_target_pairs={{0,112},{16,0},{32,16},{48,32},{64,48},{80,64},{96,80},{112,96},{1... | collective-permute-start | bytes 3145736 | tf_op jit(solution)/shard_map/ppermute | solution.py:22
  57.5 14.5 %collective-permute-start.3 = (bf16[512,1024]{1,0:T(8,128)(2,1)}, bf16[512,1024]{1,0:T(8,128)(2,1)}, u32[]{:S(2)}, u32[]{:S(2)}) collective-permute-start(bf16[512,1024]{1,0:T(8,128)(2,1)} %collective-permute-done.2), channel_id=1, source_target_pairs={{0,16},{16,32},{32,48},{48,64},{64,80},{80,96},{96,112},{112,0},{1... | collective-permute-start | bytes 3145736 | tf_op jit(solution)/shard_map/ppermute | solution.py:20
  62.6 22.9 %copy-start = (f32[256,4096]{1,0:T(8,128)}, f32[256,4096]{1,0:T(8,128)S(1)}, u32[]{:S(2)}) copy-start(f32[256,4096]{1,0:T(8,128)S(1)} %get-tuple-element.2) | copy-start | bytes 12582916
  62.6 22.9 %copy-start.1 = (f32[256,4096]{1,0:T(8,128)}, f32[256,4096]{1,0:T(8,128)S(1)}, u32[]{:S(2)}) copy-start(f32[256,4096]{1,0:T(8,128)S(1)} %get-tuple-element.3) | copy-start | bytes 12582916
  62.6 22.9 %copy-start.3 = (f32[2,1,256,1024]{3,2,1,0:T(8,128)S(1)}, f32[2,1,256,1024]{3,2,1,0:T(8,128)}, u32[]{:S(2)}) copy-start(f32[2,1,256,1024]{3,2,1,0:T(8,128)} %param.5) | copy-start | bytes 6291460
  116.5 453.7 %reduce-scatter.5.cloned.1.call-start = ((), (), s32[]{:S(2)}) async-start(), calls=%async_computation.4 | async-start | bytes 17039360 | tf_op jit(solution)/shard_map/reduce_scatter | solution.py:59
Sparse Core Ops, SparseCore 0:
  9.7 30.1 all-gather.1
  116.6 83.7 reduce-scatter.2
  203.4 366.7 reduce-scatter.4
